TPU v7x, 256 devices: a whole 4x4x8 slice. The times are simulated.
256 devices in a mesh: tensor: 2 (over core), row: 16 (over x, y), col: 8 (over z).
Axes of the slice: x: 4, y: 4, z: 8, core: 2. Of those that a mesh axis runs over, the one named last changes fastest.
Arguments:
- integral_tiles: bfloat16 [8192, 8, 4096], P(('tensor', 'row', 'col')), may hold values from -6 to 6
- tile_index: int32 [8192, 3], P(('tensor', 'row', 'col')), may hold values from 0 to 127, as said below
- virtual_coeff: bfloat16 [8192, 2048], P('col'), may hold values from -0.09375 to 0.09375
- occupied_coeff: bfloat16 [2048, 512], P('row'), may hold values from -0.125 to 0.125
Outputs:
- pair_tensor: bfloat16 [2048, 32, 512], P(('row', 'col'), 'tensor')
Inputs may be any that keep to these rules, and one draw needn't show every extreme that they name: `tile_index`: the tiles of the device at index (t, r, c) of tensor, row, col all have their nu block in c * 16 .. (c + 1) * 16 - 1, their auxiliary block below 4 and their mu block below 32. A tile's owner is (tensor index a // 2, row index m // 2) in the same col. Each device holds at most 2 tiles for any one owner; in every draw some owner gets exactly 2 tiles from every device of its col. Tiles with equal indices may occur and add up.
All inputs are finite; a program needn't handle non-finite values.
Results may differ from a plain program's by a relative error of at most 0.025.
Values may be sent and summed in bfloat16 or wider, within the bound.
No kernel may reach another device: no remote copies, remote signals or barrier semaphores. Data moves between devices by JAX's collectives and lax.ppermute only.
A program may use at most 128 MiB of HBM per device.

v0:
```python
import jax
import jax.numpy as jnp
from jax import lax
from jax.sharding import PartitionSpec as P

TB = 64
PB = 8
AB = 2
MB = 2
NBC = 16
CAP = 2
NV = 2048
NOCC = 512


def shards(integral_tiles, tile_index, virtual_coeff, occupied_coeff):
    tensor_at = lax.axis_index("tensor")
    row_at = lax.axis_index("row")
    col_at = lax.axis_index("col")
    tensor_count = lax.axis_size("tensor")
    row_count = lax.axis_size("row")
    col_count = lax.axis_size("col")
    held = integral_tiles.shape[0]
    aux_blocks = tensor_count * AB
    mu_blocks = row_count * MB
    quarters = tensor_count * 2
    qsize = TB // quarters
    assert row_count == 2 * PB and quarters * qsize == TB
    tiles = integral_tiles.reshape(held, PB, 2, tensor_count, qsize, TB)
    send = tiles.transpose(3, 1, 2, 0, 4, 5).reshape(tensor_count * row_count, held, qsize * TB)
    recv = lax.all_to_all(send, ("tensor", "row"), split_axis=0, concat_axis=0, tiled=True)
    recv = recv.reshape(tensor_count * row_count * held, qsize * TB)
    index = lax.all_gather(tile_index, ("tensor", "row"), axis=0, tiled=True)
    local_nu = index[:, 2] - col_at * NBC
    block = (index[:, 0] * NBC + local_nu) * mu_blocks + index[:, 1]
    blocks = aux_blocks * NBC * mu_blocks
    selector = (jnp.arange(blocks)[:, None] == block[None, :]).astype(jnp.bfloat16)
    dense = jnp.dot(selector, recv, preferred_element_type=jnp.float32).astype(jnp.bfloat16)
    dense = dense.reshape(aux_blocks, NBC, mu_blocks, qsize, TB)
    occ_all = lax.all_gather(occupied_coeff, "row", axis=0, tiled=True)
    quarter = 2 * (row_at % 2) + tensor_at
    occ_q = lax.dynamic_index_in_dim(
        occ_all.reshape(mu_blocks, quarters, qsize, NOCC), quarter, axis=1, keepdims=False
    )
    partial = jnp.einsum("anmuw,mui->anwi", dense, occ_q, preferred_element_type=jnp.float32)
    pair = lax.psum_scatter(partial.astype(jnp.bfloat16), "tensor", scatter_dimension=0, tiled=True)
    side = row_at % 2
    keep = lax.dynamic_index_in_dim(pair, side, axis=0, keepdims=False)
    give = lax.dynamic_index_in_dim(pair, 1 - side, axis=0, keepdims=False)
    got = lax.ppermute(give, "row", perm=[(i, i ^ 1) for i in range(row_count)])
    occ_done = (keep.astype(jnp.float32) + got.astype(jnp.float32)).astype(jnp.bfloat16)
    chunk = NV // (row_count * col_count)
    virt = virtual_coeff.reshape(NBC, TB, row_count, col_count, chunk)
    z = jnp.einsum("nwi,nwrcj->crji", occ_done, virt, preferred_element_type=jnp.float32)
    z = z.astype(jnp.bfloat16).reshape(col_count * row_count * chunk, NOCC)
    w = lax.psum_scatter(z, "col", scatter_dimension=0, tiled=True).reshape(row_count, chunk, NOCC)
    got_rows = lax.all_to_all(w, "row", split_axis=0, concat_axis=0, tiled=True)
    out = got_rows.reshape(PB, 2, chunk, NOCC).transpose(2, 1, 0, 3)
    return out.reshape(chunk, AB * PB, NOCC)


def solution(mesh):
    in_specs = (
        P(("tensor", "row", "col"), None, None),
        P(("tensor", "row", "col"), None),
        P("col", None),
        P("row", None),
    )
    out_specs = P(("row", "col"), "tensor", None)
    return jax.shard_map(shards, mesh=mesh, in_specs=in_specs, out_specs=out_specs, check_vma=False)
```

profile of v0, /device:TPU:32, one launch (start us, length us, event | category | flops | bytes accessed | tf_op | source)
XLA Modules:
  0.0 265.2 jit_solution(8073186442823905420)
XLA Ops:
  6.5 0.0 all-gather.3.cloned.1.call-start
  6.5 0.7 all-gather.3.cloned.1.call-update
  7.3 6.9 %reshape.57 = bf16[32,8,2,2,16,64]{5,4,3,2,1,0:T(8,128)(2,1)} reshape(bf16[32,8,4096]{2,1,0:T(8,128)(2,1)} %param.4) | data formatting | bytes 4194304 | tf_op jit(solution)/shard_map/reshape | solution.py:29
  14.2 5.3 %copy.42 = bf16[32,8,2,2,16,64]{5,4,0,2,1,3:T(8,128)(2,1)} copy(bf16[32,8,2,2,16,64]{5,4,3,2,1,0:T(8,128)(2,1)} %reshape.57) | data formatting | bytes 4194304 | tf_op jit(solution)/shard_map/reshape | solution.py:29
  19.5 0.0 copy-start.1
  19.5 6.5 %reshape.58 = bf16[32,32,1024]{2,1,0:T(8,128)(2,1)} reshape(bf16[2,8,2,32,16,64]{5,4,3,2,1,0:T(8,128)(2,1)} %bitcast.55) | data formatting | bytes 4194304 | tf_op jit(solution)/shard_map/reshape | solution.py:30
  26.0 7.3 %all-to-all-start = ((bf16[32,32,1024]{2,1,0:T(8,128)(2,1)}), bf16[32,32,1024]{2,1,0:T(8,128)(2,1)S(1)}, u32[]{:S(2)}, u32[]{:S(2)}) async-start(bf16[32,32,1024]{2,1,0:T(8,128)(2,1)} %reshape.58), calls=%async_computation | async-start | bytes 4194304 | tf_op jit(solution)/shard_map/all_to_all | solution.py:31
  33.4 0.0 reduce-scatter.3.cloned.1.call-start
  33.4 0.0 copy-done.1
  33.5 86.8 %all-gather = s32[32,32,3]{1,2,0:T(4,128)S(1)} all-gather(s32[1,32,3]{1,2,0:T(4,128)S(1)} %bitcast.62), channel_id=1, replica_groups=mesh['tensor'=2,'row'=16,'col'=8] {'tensor','row'}, dimensions={0}, use_global_device_ids=true | all-gather | bytes 12672 | tf_op jit(solution)/shard_map/all_gather | solution.py:33
  120.3 0.1 reshape.69
  120.4 0.0 all-to-all-done
  120.4 6.0 %fusion.4 = bf16[2048,1024]{1,0:T(8,128)(2,1)} fusion(bf16[1024,1024]{1,0:T(8,128)(2,1)S(1)} %bitcast.57, s32[1024]{0:T(1024)S(1)} %bitcast.61), kind=kOutput, calls=%fused_computation.8 | convolution fusion | flops 4299161600 | bytes 6295552 | tf_op jit(solution)/shard_map/dot_general | solution.py:38
  126.4 11.6 %reshape.60 = bf16[4,16,32,16,64]{4,3,2,1,0:T(8,128)(2,1)} reshape(bf16[2048,1024]{1,0:T(8,128)(2,1)} %fusion.4) | data formatting | bytes 8388608 | tf_op jit(solution)/shard_map/reshape | solution.py:39
  138.0 0.0 all-gather.3.cloned.1.call-done
  138.0 7.8 %bitcast_convert_fusion = bf16[4,16,64,512]{3,2,1,0:T(8,128)(2,1)} fusion(bf16[4,16,32,16,64]{4,3,2,1,0:T(8,128)(2,1)} %reshape.60, bf16[32,4,16,512]{3,2,1,0:T(8,128)(2,1)} %bitcast.60, s32[]{:T(128)S(6)} %select_n.21), kind=kOutput, calls=%fused_computation | convolution fusion | flops 2149580800 | bytes 13107204 | tf_op jit(solution)/shard_map/anmuw,mui->anwi/dot_general | solution.py:45
  145.8 0.0 reduce-scatter.3.cloned.1.call-update
  145.8 0.0 reduce-scatter.5.cloned.1.call-start
  145.9 17.0 %reduce-scatter.3.cloned.1.call-done = bf16[2,16,64,512]{3,2,1,0:T(8,128)(2,1)} async-done(((bf16[4,16,64,512]{3,2,1,0:T(8,128)(2,1)}), bf16[2,16,64,512]{3,2,1,0:T(8,128)(2,1)}) %reduce-scatter.3.cloned.1.call-update) | async-done | bytes 2097168 | tf_op jit(solution)/shard_map/reduce_scatter | solution.py:46
  162.9 1.3 dynamic-slice_bitcast_fusion
  164.2 1.7 collective-permute-start
  165.9 6.4 %copy.25 = bf16[1024,2048]{0,1:T(8,128)(2,1)} copy(bf16[1024,2048]{1,0:T(8,128)(2,1)} %param.6) | data formatting | bytes 8388608 | tf_op args[2]
  172.3 0.0 copy-start
  172.3 11.8 %reshape.62 = bf16[16,64,16,8,16]{1,0,4,3,2:T(8,128)(2,1)} reshape(bf16[1024,2048]{0,1:T(8,128)(2,1)} %copy.25) | data formatting | bytes 8388608 | tf_op jit(solution)/shard_map/reshape | solution.py:53
  184.1 5.8 %collective-permute-done = bf16[16,64,512]{2,1,0:T(8,128)(2,1)} collective-permute-done((bf16[16,64,512]{2,1,0:T(8,128)(2,1)S(1)}, bf16[16,64,512]{2,1,0:T(8,128)(2,1)}, u32[]{:S(2)}, u32[]{:S(2)}) %collective-permute-start) | collective-permute-done | bytes 1048608 | tf_op jit(solution)/shard_map/ppermute | solution.py:50
  189.8 0.0 copy-done
  189.8 8.0 %fusion.8 = bf16[8,16,16,512]{3,2,0,1:T(8,128)(2,1)S(1)} fusion(bf16[16,64,16,8,16]{1,0,4,3,2:T(8,128)(2,1)} %reshape.62, bf16[16,64,512]{2,1,0:T(8,128)(2,1)} %collective-permute-done, bf16[2,16,64,512]{3,2,1,0:T(8,128)(2,1)S(1)} %copy-done, s32[]{:T(128)S(6)} %select_n.22), kind=kOutput, calls=%fused_computation.11 | convolution fusion | flops 2150629376 | bytes 8388612 | tf_op jit(solution)/shard_map/nwi,nwrcj->crji/dot_general | solution.py:54
  197.8 1.5 copy.27
  199.3 0.0 reduce-scatter.5.cloned.1.call-update
  199.4 42.9 %reduce-scatter.5.cloned.1.call-done = bf16[256,512]{1,0:T(8,128)(2,1)} async-done(((bf16[2048,512]{1,0:T(8,128)(2,1)}), bf16[256,512]{1,0:T(8,128)(2,1)}) %reduce-scatter.5.cloned.1.call-update) | async-done | bytes 262160 | tf_op jit(solution)/shard_map/reduce_scatter | solution.py:56
  242.3 15.5 %all_to_all.10 = bf16[16,16,512]{2,1,0:T(8,128)(2,1)S(1)} all-to-all(bf16[16,16,512]{2,1,0:T(8,128)(2,1)} %bitcast.59), channel_id=1, replica_groups=mesh['tensor'=2,'row'=16,'col'=8] {'row'}, dimensions={0} | all-to-all | bytes 524288 | tf_op jit(solution)/shard_map/all_to_all | solution.py:57
  257.8 0.9 copy.43
  (2 shorter events, 0.0 us)
Async XLA Ops:
  6.5 131.5 %all-gather.3.cloned.1.call-start = ((), (), s32[]{:S(2)}) async-start(), calls=%async_computation.4 | async-start | bytes 2228224 | tf_op jit(solution)/shard_map/all_gather | solution.py:40
  19.5 13.9 %copy-start.1 = (s32[32,3]{0,1:T(4,128)S(1)}, s32[32,3]{0,1:T(4,128)}, u32[]{:S(2)}) copy-start(s32[32,3]{0,1:T(4,128)} %param.5) | copy-start | bytes 1156
  26.0 94.3 %all-to-all-start = ((bf16[32,32,1024]{2,1,0:T(8,128)(2,1)}), bf16[32,32,1024]{2,1,0:T(8,128)(2,1)S(1)}, u32[]{:S(2)}, u32[]{:S(2)}) async-start(bf16[32,32,1024]{2,1,0:T(8,128)(2,1)} %reshape.58), calls=%async_computation | async-start | bytes 4194304 | tf_op jit(solution)/shard_map/all_to_all | solution.py:31
  33.4 129.5 %reduce-scatter.3.cloned.1.call-start = ((), (), s32[]{:S(2)}) async-start(), calls=%async_computation.5 | async-start | bytes 6291456 | tf_op jit(solution)/shard_map/reduce_scatter | solution.py:46
  145.8 96.5 %reduce-scatter.5.cloned.1.call-start = ((), (), s32[]{:S(2)}) async-start(), calls=%async_computation.6 | async-start | bytes 2359296 | tf_op jit(solution)/shard_map/reduce_scatter | solution.py:56
  164.2 25.6 %collective-permute-start = (bf16[16,64,512]{2,1,0:T(8,128)(2,1)S(1)}, bf16[16,64,512]{2,1,0:T(8,128)(2,1)}, u32[]{:S(2)}, u32[]{:S(2)}) collective-permute-start(bf16[16,64,512]{2,1,0:T(8,128)(2,1)S(1)} %dynamic-slice_bitcast_fusion), channel_id=1, source_target_pairs={{0,8},{8,0},{16,24},{24,16},{32,40},{40,32},{48,56},{56,48},{64,72... | collective-permute-start | bytes 3145736 | tf_op jit(solution)/shard_map/ppermute | solution.py:50
  172.3 17.5 %copy-start = (bf16[2,16,64,512]{3,2,1,0:T(8,128)(2,1)S(1)}, bf16[2,16,64,512]{3,2,1,0:T(8,128)(2,1)}, u32[]{:S(2)}) copy-start(bf16[2,16,64,512]{3,2,1,0:T(8,128)(2,1)} %reduce-scatter.3.cloned.1.call-done) | copy-start | bytes 6291460
Sparse Core Ops, SparseCore 0:
  9.8 63.4 all-gather.2
  145.9 16.8 reduce-scatter.2
  199.5 42.7 reduce-scatter.4
where the time goes:
time: 266 us; the launch traced here: 265 us
  blocking collectives  102 us (38%)
  waiting for transfers between devices  66.4 us (25%)
  local copies, waits for them, and re-layouts  52.3 us (20%)
  matrix products  21.8 us (8%)
  between operations  13.2 us (5%)
  starting transfers between devices  9.15 us (3%)
    all_gather x1, blocking collectives, shards(): index = lax.all_gather(tile_index, ('tensor', 'row'), axis=0, tiled=True)  86.8 us
    reduce_scatter x1, waiting for transfers between devices, shards(): lax.psum_scatter(z, 'col', scatter_dimension=0, tiled=True)  42.9 us
    reduce_scatter x1, waiting for transfers between devices, shards(): lax.psum_scatter(partial.astype(jnp.bfloat16), 'tensor', scatter_dimensio...  17 us
    all_to_all x1, blocking collectives, shards(): got_rows = lax.all_to_all(w, 'row', split_axis=0, concat_axis=0, tiled=True)  15.5 us
    reshape x2, local copies, waits for them, and re-layouts, shards(): tiles = integral_tiles.reshape(held, PB, 2, tensor_count, qsize, TB)  12.3 us
    reshape x1, local copies, waits for them, and re-layouts, shards(): virt = virtual_coeff.reshape(NBC, TB, row_count, col_count, chunk)  11.8 us
    reshape x1, local copies, waits for them, and re-layouts, shards(): dense = dense.reshape(aux_blocks, NBC, mu_blocks, qsize, TB)  11.6 us
    dot_general x1, matrix products, shards(): jnp.einsum('nwi,nwrcj->crji', occ_done, virt, preferred_element_type=jnp....  7.97 us
  transfers between devices with their start and end apart: 5, of which 3 were waited for; matrix products, arithmetic and copies ran while one was open for 21% of the time, Pallas kernels for 0%

commit v1 on v0

--- a/solution.py
+++ b/solution.py
@@ -30,7 +30,11 @@
     send = tiles.transpose(3, 1, 2, 0, 4, 5).reshape(tensor_count * row_count, held, qsize * TB)
     recv = lax.all_to_all(send, ("tensor", "row"), split_axis=0, concat_axis=0, tiled=True)
     recv = recv.reshape(tensor_count * row_count * held, qsize * TB)
-    index = lax.all_gather(tile_index, ("tensor", "row"), axis=0, tiled=True)
+    devices = lax.axis_size(("tensor", "row"))
+    repeats = [devices if d == 0 else 1 for d in range(tile_index.ndim)]
+    index = lax.all_to_all(
+        jnp.tile(tile_index, repeats), ("tensor", "row"), split_axis=0, concat_axis=0, tiled=True
+    )
     local_nu = index[:, 2] - col_at * NBC
     block = (index[:, 0] * NBC + local_nu) * mu_blocks + index[:, 1]
     blocks = aux_blocks * NBC * mu_blocks

time: 266 us -> 225 us (0.85)
  blocking collectives: 102 us -> 15.2 us
  waiting for transfers between devices: 66.4 us -> 104 us
  starting transfers between devices: 9.15 us -> 16.5 us
    all_gather x1 -> x0, blocking collectives: 86.8 us -> none  [shards(): index = lax.all_gather(tile_index, ('tensor', 'row'), axis=0, tiled=True)]
    all_to_all x1, waiting for transfers between devices: 0.01 us -> 35.3 us  [shards(): lax.all_to_all(send, ('tensor', 'row'), split_axis=0, concat_axis=0, tile...]
    all_to_all x0 -> x1, starting transfers between devices: none -> 7.32 us  [shards(): lax.all_to_all(jnp.tile(tile_index, repeats), ('tensor', 'row'), split_ax...]
    unnamed x6 -> x3, local copies, waits for them, and re-layouts: 6.47 us -> 6.4 us
  transfers between devices with their start and end apart: 5 -> 6, of which waited for: 3 -> 4; matrix products, arithmetic and copies ran while one was open for 21% -> 25% of each run, Pallas kernels for 0% -> 0%
where the time goes in v1:
time: 225 us; the launch traced here: 224 us
  waiting for transfers between devices  104 us (46%)
  local copies, waits for them, and re-layouts  53.7 us (24%)
  matrix products  21.8 us (10%)
  starting transfers between devices  16.5 us (7%)
  blocking collectives  15.2 us (7%)
  between operations  13.2 us (6%)
    reduce_scatter x1, waiting for transfers between devices, shards(): lax.psum_scatter(z, 'col', scatter_dimension=0, tiled=True)  43.2 us
    all_to_all x1, waiting for transfers between devices, shards(): lax.all_to_all(send, ('tensor', 'row'), split_axis=0, concat_axis=0, tile...  35.3 us
    reduce_scatter x1, waiting for transfers between devices, shards(): lax.psum_scatter(partial.astype(jnp.bfloat16), 'tensor', scatter_dimensio...  18.6 us
    all_to_all x1, blocking collectives, shards(): got_rows = lax.all_to_all(w, 'row', split_axis=0, concat_axis=0, tiled=True)  15.2 us
    reshape x2, local copies, waits for them, and re-layouts, shards(): tiles = integral_tiles.reshape(held, PB, 2, tensor_count, qsize, TB)  12.3 us
    reshape x1, local copies, waits for them, and re-layouts, shards(): virt = virtual_coeff.reshape(NBC, TB, row_count, col_count, chunk)  11.7 us
    reshape x1, local copies, waits for them, and re-layouts, shards(): dense = dense.reshape(aux_blocks, NBC, mu_blocks, qsize, TB)  11.6 us
    dot_general x1, matrix products, shards(): jnp.einsum('nwi,nwrcj->crji', occ_done, virt, preferred_element_type=jnp....  7.97 us
  transfers between devices with their start and end apart: 6, of which 4 were waited for; matrix products, arithmetic and copies ran while one was open for 25% of the time, Pallas kernels for 0%

profile of v1, /device:TPU:32, one launch (start us, length us, event | category | flops | bytes accessed | tf_op | source)
XLA Modules:
  0.0 223.9 jit_solution(2024560122701207661)
XLA Ops:
  6.5 0.0 all-gather.2.cloned.1.call-start
  6.5 0.7 all-gather.2.cloned.1.call-update
  7.3 1.3 tile.2
  8.6 7.3 %all-to-all-start = ((s32[32,32,3]{1,2,0:T(4,128)}), s32[32,32,3]{1,2,0:T(4,128)S(1)}, u32[]{:S(2)}, u32[]{:S(2)}) async-start(s32[32,32,3]{1,2,0:T(4,128)} %tile.2), calls=%async_computation | async-start | bytes 131072 | tf_op jit(solution)/shard_map/all_to_all | solution.py:35
  15.9 6.9 %reshape.64 = bf16[32,8,2,2,16,64]{5,4,3,2,1,0:T(8,128)(2,1)} reshape(bf16[32,8,4096]{2,1,0:T(8,128)(2,1)} %param.4) | data formatting | bytes 4194304 | tf_op jit(solution)/shard_map/reshape | solution.py:29
  22.8 5.4 %copy.47 = bf16[32,8,2,2,16,64]{5,4,0,2,1,3:T(8,128)(2,1)} copy(bf16[32,8,2,2,16,64]{5,4,3,2,1,0:T(8,128)(2,1)} %reshape.64) | data formatting | bytes 4194304 | tf_op jit(solution)/shard_map/reshape | solution.py:29
  28.2 6.5 %reshape.65 = bf16[32,32,1024]{2,1,0:T(8,128)(2,1)} reshape(bf16[2,8,2,32,16,64]{5,4,3,2,1,0:T(8,128)(2,1)} %bitcast.54) | data formatting | bytes 4194304 | tf_op jit(solution)/shard_map/reshape | solution.py:30
  34.7 0.0 all-to-all-done
  34.7 7.4 %all-to-all-start.1 = ((bf16[32,32,1024]{2,1,0:T(8,128)(2,1)}), bf16[32,32,1024]{2,1,0:T(8,128)(2,1)S(1)}, u32[]{:S(2)}, u32[]{:S(2)}) async-start(bf16[32,32,1024]{2,1,0:T(8,128)(2,1)} %reshape.65), calls=%async_computation.1 | async-start | bytes 4194304 | tf_op jit(solution)/shard_map/all_to_all | solution.py:31
  42.1 0.0 reduce-scatter.3.cloned.1.call-start
  42.2 0.1 all_to_all.13
  42.3 35.3 %all-to-all-done.1 = bf16[32,32,1024]{2,1,0:T(8,128)(2,1)S(1)} async-done(((bf16[32,32,1024]{2,1,0:T(8,128)(2,1)}), bf16[32,32,1024]{2,1,0:T(8,128)(2,1)S(1)}, u32[]{:S(2)}, u32[]{:S(2)}) %all-to-all-start.1) | async-done | bytes 2097184 | tf_op jit(solution)/shard_map/all_to_all | solution.py:31
  77.7 6.0 %fusion.4 = bf16[2048,1024]{1,0:T(8,128)(2,1)} fusion(bf16[1024,1024]{1,0:T(8,128)(2,1)S(1)} %bitcast.56, s32[1024]{0:T(1024)S(1)} %bitcast.60), kind=kOutput, calls=%fused_computation.8 | convolution fusion | flops 4299161600 | bytes 6295552 | tf_op jit(solution)/shard_map/dot_general | solution.py:42
  83.7 11.6 %reshape.67 = bf16[4,16,32,16,64]{4,3,2,1,0:T(8,128)(2,1)} reshape(bf16[2048,1024]{1,0:T(8,128)(2,1)} %fusion.4) | data formatting | bytes 8388608 | tf_op jit(solution)/shard_map/reshape | solution.py:43
  95.3 0.0 all-gather.2.cloned.1.call-done
  95.3 7.8 %bitcast_convert_fusion = bf16[4,16,64,512]{3,2,1,0:T(8,128)(2,1)} fusion(bf16[4,16,32,16,64]{4,3,2,1,0:T(8,128)(2,1)} %reshape.67, bf16[32,4,16,512]{3,2,1,0:T(8,128)(2,1)} %bitcast.59, s32[]{:T(128)S(6)} %select_n.21), kind=kOutput, calls=%fused_computation | convolution fusion | flops 2149580800 | bytes 13107204 | tf_op jit(solution)/shard_map/anmuw,mui->anwi/dot_general | solution.py:49
  103.1 0.0 reduce-scatter.3.cloned.1.call-update
  103.1 0.0 reduce-scatter.5.cloned.1.call-start
  103.1 18.6 %reduce-scatter.3.cloned.1.call-done = bf16[2,16,64,512]{3,2,1,0:T(8,128)(2,1)} async-done(((bf16[4,16,64,512]{3,2,1,0:T(8,128)(2,1)}), bf16[2,16,64,512]{3,2,1,0:T(8,128)(2,1)}) %reduce-scatter.3.cloned.1.call-update) | async-done | bytes 2097168 | tf_op jit(solution)/shard_map/reduce_scatter | solution.py:50
  121.7 1.3 dynamic-slice_bitcast_fusion
  123.0 1.7 collective-permute-start
  124.8 6.4 %copy.30 = bf16[1024,2048]{0,1:T(8,128)(2,1)} copy(bf16[1024,2048]{1,0:T(8,128)(2,1)} %param.6) | data formatting | bytes 8388608 | tf_op args[2]
  131.2 0.0 copy-start
  131.2 11.7 %reshape.69 = bf16[16,64,16,8,16]{1,0,4,3,2:T(8,128)(2,1)} reshape(bf16[1024,2048]{0,1:T(8,128)(2,1)} %copy.30) | data formatting | bytes 8388608 | tf_op jit(solution)/shard_map/reshape | solution.py:57
  142.9 5.7 %collective-permute-done = bf16[16,64,512]{2,1,0:T(8,128)(2,1)} collective-permute-done((bf16[16,64,512]{2,1,0:T(8,128)(2,1)S(1)}, bf16[16,64,512]{2,1,0:T(8,128)(2,1)}, u32[]{:S(2)}, u32[]{:S(2)}) %collective-permute-start) | collective-permute-done | bytes 1048608 | tf_op jit(solution)/shard_map/ppermute | solution.py:54
  148.7 0.0 copy-done
  148.7 8.0 %fusion.8 = bf16[8,16,16,512]{3,2,0,1:T(8,128)(2,1)S(1)} fusion(bf16[16,64,16,8,16]{1,0,4,3,2:T(8,128)(2,1)} %reshape.69, bf16[16,64,512]{2,1,0:T(8,128)(2,1)} %collective-permute-done, bf16[2,16,64,512]{3,2,1,0:T(8,128)(2,1)S(1)} %copy-done, s32[]{:T(128)S(6)} %select_n.22), kind=kOutput, calls=%fused_computation.11 | convolution fusion | flops 2150629376 | bytes 8388612 | tf_op jit(solution)/shard_map/nwi,nwrcj->crji/dot_general | solution.py:58
  156.6 1.5 copy.32
  158.2 0.0 reduce-scatter.5.cloned.1.call-update
  158.2 43.2 %reduce-scatter.5.cloned.1.call-done = bf16[256,512]{1,0:T(8,128)(2,1)} async-done(((bf16[2048,512]{1,0:T(8,128)(2,1)}), bf16[256,512]{1,0:T(8,128)(2,1)}) %reduce-scatter.5.cloned.1.call-update) | async-done | bytes 262160 | tf_op jit(solution)/shard_map/reduce_scatter | solution.py:60
  201.4 15.2 %all_to_all.19 = bf16[16,16,512]{2,1,0:T(8,128)(2,1)S(1)} all-to-all(bf16[16,16,512]{2,1,0:T(8,128)(2,1)} %bitcast.58), channel_id=1, replica_groups=mesh['tensor'=2,'row'=16,'col'=8] {'row'}, dimensions={0} | all-to-all | bytes 524288 | tf_op jit(solution)/shard_map/all_to_all | solution.py:61
  216.5 0.9 copy.48
  (2 shorter events, 0.0 us)
Async XLA Ops:
  6.5 88.7 %all-gather.2.cloned.1.call-start = ((), (), s32[]{:S(2)}) async-start(), calls=%async_computation.5 | async-start | bytes 2228224 | tf_op jit(solution)/shard_map/all_gather | solution.py:44
  8.6 26.1 %all-to-all-start = ((s32[32,32,3]{1,2,0:T(4,128)}), s32[32,32,3]{1,2,0:T(4,128)S(1)}, u32[]{:S(2)}, u32[]{:S(2)}) async-start(s32[32,32,3]{1,2,0:T(4,128)} %tile.2), calls=%async_computation | async-start | bytes 131072 | tf_op jit(solution)/shard_map/all_to_all | solution.py:35
  34.7 42.9 %all-to-all-start.1 = ((bf16[32,32,1024]{2,1,0:T(8,128)(2,1)}), bf16[32,32,1024]{2,1,0:T(8,128)(2,1)S(1)}, u32[]{:S(2)}, u32[]{:S(2)}) async-start(bf16[32,32,1024]{2,1,0:T(8,128)(2,1)} %reshape.65), calls=%async_computation.1 | async-start | bytes 4194304 | tf_op jit(solution)/shard_map/all_to_all | solution.py:31
  42.1 79.6 %reduce-scatter.3.cloned.1.call-start = ((), (), s32[]{:S(2)}) async-start(), calls=%async_computation.6 | async-start | bytes 6291456 | tf_op jit(solution)/shard_map/reduce_scatter | solution.py:50
  103.1 98.3 %reduce-scatter.5.cloned.1.call-start = ((), (), s32[]{:S(2)}) async-start(), calls=%async_computation.7 | async-start | bytes 2359296 | tf_op jit(solution)/shard_map/reduce_scatter | solution.py:60
  123.0 25.6 %collective-permute-start = (bf16[16,64,512]{2,1,0:T(8,128)(2,1)S(1)}, bf16[16,64,512]{2,1,0:T(8,128)(2,1)}, u32[]{:S(2)}, u32[]{:S(2)}) collective-permute-start(bf16[16,64,512]{2,1,0:T(8,128)(2,1)S(1)} %dynamic-slice_bitcast_fusion), channel_id=1, source_target_pairs={{0,8},{8,0},{16,24},{24,16},{32,40},{40,32},{48,56},{56,48},{64,72... | collective-permute-start | bytes 3145736 | tf_op jit(solution)/shard_map/ppermute | solution.py:54
  131.2 17.5 %copy-start = (bf16[2,16,64,512]{3,2,1,0:T(8,128)(2,1)S(1)}, bf16[2,16,64,512]{3,2,1,0:T(8,128)(2,1)}, u32[]{:S(2)}) copy-start(bf16[2,16,64,512]{3,2,1,0:T(8,128)(2,1)} %reduce-scatter.3.cloned.1.call-done) | copy-start | bytes 6291460
Sparse Core Ops, SparseCore 0:
  9.8 68.8 all-gather.1
  103.2 18.4 reduce-scatter.2
  158.3 43.0 reduce-scatter.4
